TPU v7x, 32 devices: a whole 2x2x4 slice. The times are simulated.
32 devices in a mesh: grp: 8 (over z, x), rep: 4 (over y, core).
Axes of the slice: x: 2, y: 2, z: 4, core: 2. Of those that a mesh axis runs over, the one named last changes fastest.
Arguments:
- three_center: bfloat16 [4, 64, 32, 6, 4096], P('rep', 'grp'), may hold values from -2 to 2
- metric: bfloat16 [4, 64, 64], P('rep'), may hold values from -0.75 to 0.75
- occupied: bfloat16 [2048, 48], replicated, may hold values from -0.3125 to 0.3125
- nu_list: int32 [32, 6], replicated, may hold values from 0 to 31, as said below
- nu_count: int32 [32], replicated, may hold values from 1 to 6
- block_size: int32 [32], replicated, may hold values from 32 to 64
Outputs:
- exchange_matrix: float32 [2048, 2048], P('rep', 'grp')
Inputs may be any that keep to these rules, and one draw needn't show every extreme that they name: `nu_list`: entry 0 of row m is m itself; the other entries of a row are distinct blocks other than m.
All inputs are finite; a program needn't handle non-finite values.
Results may differ from a plain program's by a relative error of at most 0.0024.
Values may be sent and summed in bfloat16 or wider, within the bound.
No kernel may reach another device: no remote copies, remote signals or barrier semaphores. Data moves between devices by JAX's collectives and lax.ppermute only.
A program may use at most 192 MiB of HBM per device.

v0:
```python
import jax
import jax.numpy as jnp
import numpy as np
from jax import lax
from jax.sharding import PartitionSpec as P

NB = 64


def snake(a_size, b_size):
    if a_size % 2:
        return [(a, b) for b, a in snake(b_size, a_size)]
    if b_size == 1:
        return [(a, 0) for a in range(a_size)]
    path = []
    for a in range(a_size):
        cols = (
            range(b_size)
            if a == 0
            else range(1, b_size) if a % 2 == 0 else range(b_size - 1, 0, -1)
        )
        path += [(a, b) for b in cols]
    path += [(a, 0) for a in range(a_size - 1, 0, -1)]
    return path


def ring_order(mesh):
    n = mesh.shape["grp"]
    try:
        devs = np.asarray(mesh.devices).reshape(n, -1)[:, 0]
        coords = [tuple(d.coords) for d in devs]
    except (AttributeError, TypeError):
        return list(range(n))
    varying = [i for i in range(len(coords[0])) if len({c[i] for c in coords}) > 1]
    if len(varying) == 1:
        key = sorted(range(n), key=lambda g: coords[g][varying[0]])
        return key
    if len(varying) != 2:
        return list(range(n))
    i, j = varying
    avals = sorted({c[i] for c in coords})
    bvals = sorted({c[j] for c in coords})
    where = {(avals.index(c[i]), bvals.index(c[j])): g for g, c in enumerate(coords)}
    if len(where) != n:
        return list(range(n))
    return [where[p] for p in snake(len(avals), len(bvals))]


def scatter_sum(term):
    n_rep = lax.axis_size("rep")
    if n_rep & n_rep - 1:
        return lax.psum_scatter(term, "rep", scatter_dimension=0, tiled=True)
    me = lax.axis_index("rep")
    bits = n_rep.bit_length() - 1
    per = term.shape[0] // n_rep
    buf = term.reshape((2,) * bits + (per,) + term.shape[1:])
    for b in range(bits):
        d = 1 << b
        axis = buf.ndim - 3
        mine = me // d % 2
        keep = lax.dynamic_index_in_dim(buf, mine, axis=axis, keepdims=False)
        send = lax.dynamic_index_in_dim(buf, 1 - mine, axis=axis, keepdims=False)
        got = lax.ppermute(send, "rep", [(i, i ^ d) for i in range(n_rep)])
        buf = keep + got
    return buf.reshape(per, term.shape[1])


def make_body(ring):
    n = len(ring)
    pos_of = np.zeros(n, np.int32)
    for p, g in enumerate(ring):
        pos_of[g] = p
    ring_arr = np.asarray(ring, np.int32)

    def shifted(s):
        return [(ring[p], ring[(p + s) % n]) for p in range(n)]

    def body(three_center, metric, occupied, nu_list, nu_count, block_size):
        n_mu, knu = nu_list.shape
        n_occ = occupied.shape[1]
        aux_dev = three_center.shape[1]
        lanes = jnp.arange(NB, dtype=jnp.int32)
        row_live = lanes[None, :] < block_size[:, None]
        col_live = lanes[None, None, :] < block_size[nu_list][:, :, None]
        slot_live = jnp.arange(knu, dtype=jnp.int32)[None, :] < nu_count[:, None]
        keep = col_live & slot_live[:, :, None]
        picked = occupied.reshape(n_mu, NB, n_occ)[nu_list]
        picked = jnp.where(keep[..., None], picked, jnp.zeros((), jnp.bfloat16))
        pair = 2
        blank = jnp.zeros_like(picked)
        weight = jnp.concatenate(
            [jnp.concatenate([picked, blank], axis=-1), jnp.concatenate([blank, picked], axis=-1)],
            axis=-2,
        )
        tiles = NB // pair
        tc = jnp.swapaxes(three_center[0], 1, 2).reshape(aux_dev, knu, n_mu, tiles, pair * NB)
        half = jnp.einsum("qkmtl,mklc->qmtc", tc, weight, preferred_element_type=jnp.float32)
        half = half.reshape(aux_dev, n_mu, NB, n_occ)
        half = jnp.where(row_live[None, :, :, None], half, 0.0).astype(jnp.bfloat16)
        mu_dev = n_mu // n
        n_split = 2 if mu_dev % 2 == 0 else 1
        mu_c = mu_dev // n_split
        half = half.reshape(aux_dev, n, mu_dev, NB * n_occ)
        me = lax.axis_index("grp")
        pos = jnp.asarray(pos_of)[me]
        ring_c = jnp.asarray(ring_arr)
        radius = n // 4
        helds = []
        for h in range(n_split):
            part = half[:, :, h * mu_c : (h + 1) * mu_c].reshape(aux_dev, n * mu_c, NB * n_occ)
            regrouped = lax.all_to_all(part, "grp", split_axis=1, concat_axis=0, tiled=True)
            n_aux = regrouped.shape[0]
            mixed = jnp.dot(
                metric[0], regrouped.reshape(n_aux, -1), preferred_element_type=jnp.float32
            )
            mixed = mixed.astype(jnp.bfloat16).reshape(n_aux, mu_c, NB, n_occ)
            orbital = jnp.transpose(mixed, (1, 2, 0, 3)).reshape(mu_c * NB, n_aux * n_occ)
            held = {0: orbital}
            fwd = orbital
            bwd = orbital
            for k in range(1, radius + 1):
                fwd = lax.ppermute(fwd, "grp", shifted(1))
                held[-k] = fwd
                bwd = lax.ppermute(bwd, "grp", shifted(-1))
                held[k] = bwd
            helds.append(held)
        held = {off: jnp.concatenate([hd[off] for hd in helds], axis=0) for off in helds[0]}
        rows = mu_dev * NB

        def start_of(off):
            return ring_c[(pos + off) % n] * rows

        def prod(xo, yo):
            return jnp.dot(held[xo], held[yo].T, preferred_element_type=jnp.float32)

        local = []
        outgoing = {}
        for d in range(n // 2 + 1):
            xo = -((d + 1) // 2)
            yo = xo + d
            blk = prod(xo, yo)
            s = d // 2
            if s == 0:
                local.append((-d, blk))
            else:
                outgoing.setdefault(s, []).append((-d, blk))
            if 0 < d < n // 2:
                outgoing.setdefault(xo, []).append((d, blk.T))
        placed = list(local)
        for s, items in sorted(outgoing.items()):
            stack = jnp.stack([b for _, b in items])
            got = lax.ppermute(stack, "grp", shifted(s))
            placed += [(off, got[i]) for i, (off, _) in enumerate(items)]
        term = jnp.zeros((n * rows, rows), jnp.float32)
        for off, blk in placed:
            term = lax.dynamic_update_slice_in_dim(term, blk, start_of(off), axis=0)
        return scatter_sum(term)

    return body


def solution(mesh):
    return jax.shard_map(
        make_body(ring_order(mesh)),
        mesh=mesh,
        in_specs=(P("rep", "grp", None, None, None), P("rep", None, None), P(), P(), P(), P()),
        out_specs=P("rep", "grp"),
        check_vma=False,
    )
```

profile of v0, /device:TPU:2, one launch (start us, length us, event | category | flops | bytes accessed | tf_op | source)
XLA Modules:
  0.0 207.9 jit_solution(4243646130246210751)
XLA Ops:
  0.9 1.3 reshape.104
  3.2 1.6 gather_fusion
  4.7 1.0 gather_fusion.1
  5.9 7.4 %copy.30 = bf16[192,8,32,128]{3,2,1,0:T(8,128)(2,1)S(1)} copy(bf16[192,8,32,128]{3,1,2,0:T(8,128)(2,1)} %bitcast.112) | data formatting | bytes 25165824
  13.5 1.7 broadcast_select_fusion
  15.1 7.2 %fusion.14 = bf16[8,32,32,96]{3,2,0,1:T(8,128)(2,1)} fusion(bf16[8,6,32,32,128]{4,3,2,1,0:T(8,128)(2,1)S(1)} %bitcast.113, bf16[32,6,64,48]{2,3,1,0:T(8,128)(2,1)} %broadcast_select_fusion), kind=kOutput, calls=%fused_computation.20 | convolution fusion | flops 1226833920 | bytes 15335424 | tf_op jit(solution)/shard_map/qkmtl,mklc->qmtc/dot_general | solution.py:97
  22.3 4.2 %reshape.106 = bf16[8,8,4,3072]{3,0,2,1:T(8,128)(2,1)S(1)} reshape(bf16[8,32,32,96]{3,2,0,1:T(8,128)(2,1)} %fusion.14) | data formatting | bytes 3145728 | tf_op jit(solution)/shard_map/reshape | solution.py:98
  28.1 1.0 fusion.35
  29.1 25.8 %all_to_all.30 = bf16[8,16,3072]{2,0,1:T(8,128)(2,1)S(1)} all-to-all(bf16[8,16,3072]{2,0,1:T(8,128)(2,1)S(1)} %bitcast.120), channel_id=1, replica_groups=mesh['grp'=8,'rep'=4] {'grp'}, dimensions={1} | all-to-all | bytes 1572864 | tf_op jit(solution)/shard_map/all_to_all | solution.py:111
  55.0 4.2 %all-to-all-start.1 = ((bf16[8,16,3072]{2,0,1:T(8,128)(2,1)}), bf16[8,16,3072]{2,0,1:T(8,128)(2,1)S(1)}, u32[]{:S(2)}, u32[]{:S(2)}) async-start(bf16[8,16,3072]{2,0,1:T(8,128)(2,1)} %bitcast.15), calls=%async_computation.1 | async-start | bytes 1572864 | tf_op jit(solution)/shard_map/all_to_all | solution.py:111
  68.2 1.2 fusion.4
  69.5 3.3 %reshape.109 = bf16[64,2,64,48]{3,2,1,0:T(8,128)(2,1)S(1)} reshape(bf16[64,6144]{1,0:T(8,128)(2,1)} %fusion.4) | data formatting | bytes 1572864 | tf_op jit(solution)/shard_map/reshape | solution.py:116
  72.7 4.2 %copy.23 = bf16[2,64,64,48]{1,0,3,2:T(2,128)(2,1)} copy(bf16[2,64,64,48]{3,1,0,2:T(8,128)(2,1)S(1)} %bitcast.116) | data formatting | bytes 1572864 | tf_op jit(solution)/shard_map/transpose | solution.py:117
  77.0 3.9 %reshape.110 = bf16[128,3072]{0,1:T(8,128)(2,1)} reshape(bf16[2,64,64,48]{1,0,3,2:T(2,128)(2,1)} %copy.23) | data formatting | bytes 1572864 | tf_op jit(solution)/shard_map/reshape | solution.py:117
  80.9 2.0 collective-permute-start.4
  82.9 2.1 %constant_dynamic-update-slice_fusion.1 = bf16[256,3072]{0,1:T(8,128)(2,1)} fusion(bf16[128,3072]{0,1:T(8,128)(2,1)} %reshape.110), kind=kLoop, calls=%fused_computation.43 | loop fusion | bytes 1572864
  85.4 2.2 %reshape.113 = bf16[64,2,64,48]{3,2,1,0:T(8,128)(2,1)S(1)} reshape(bf16[64,6144]{1,0:T(8,128)(2,1)S(1)} %fusion.5) | data formatting | bytes 1572864 | tf_op jit(solution)/shard_map/reshape | solution.py:116
  87.6 4.2 %copy.24 = bf16[2,64,64,48]{1,0,3,2:T(2,128)(2,1)} copy(bf16[2,64,64,48]{3,1,0,2:T(8,128)(2,1)S(1)} %bitcast.117) | data formatting | bytes 1572864 | tf_op jit(solution)/shard_map/transpose | solution.py:117
  91.8 3.1 %reshape.114 = bf16[128,3072]{0,1:T(8,128)(2,1)S(1)} reshape(bf16[2,64,64,48]{1,0,3,2:T(2,128)(2,1)} %copy.24) | data formatting | bytes 1572864 | tf_op jit(solution)/shard_map/reshape | solution.py:117
  95.1 2.0 collective-permute-start.5
  97.1 1.0 constant_dynamic-update-slice_fusion
  98.2 2.5 %convolution_dynamic-update-slice_fusion = f32[2048,256]{1,0:T(8,128)S(1)} fusion(f32[2048,256]{1,0:T(8,128)S(1)} %broadcast_in_dim.45, s32[]{:T(128)S(6)} %select_n.132, bf16[256,3072]{0,1:T(8,128)(2,1)} %constant_dynamic-update-slice_fusion), kind=kOutput, calls=%fused_computation.25 | convolution fusion | flops 402653184 | bytes 3407876 | tf_op jit(solution)/shard_map/dot_general | solution.py:134
  100.7 1.0 collective-permute-done
  101.7 1.3 constant_dynamic-update-slice_fusion.3
  103.0 1.3 constant_dynamic-update-slice_fusion.7
  104.2 12.2 %collective-permute-done.1 = bf16[128,3072]{0,1:T(8,128)(2,1)} collective-permute-done((bf16[128,3072]{0,1:T(8,128)(2,1)S(1)}, bf16[128,3072]{0,1:T(8,128)(2,1)}, u32[]{:S(2)}, u32[]{:S(2)}) %collective-permute-start.1) | collective-permute-done | bytes 786464 | tf_op jit(solution)/shard_map/ppermute | solution.py:122
  116.4 1.3 constant_dynamic-update-slice_fusion.2
  118.6 2.0 constant_dynamic-update-slice_fusion.11
  121.1 1.8 collective-permute-start.7
  127.0 1.8 collective-permute-start.10
  128.8 1.5 collective-permute-start.9
  130.3 5.8 %collective-permute-done.7 = f32[2,256,256]{1,2,0:T(8,128)} collective-permute-done((f32[2,256,256]{1,2,0:T(8,128)S(1)}, f32[2,256,256]{1,2,0:T(8,128)}, u32[]{:S(2)}, u32[]{:S(2)}) %collective-permute-start.7) | collective-permute-done | bytes 524320 | tf_op jit(solution)/shard_map/ppermute | solution.py:152
  136.1 1.1 slice_bitcast_fusion.2
  137.5 4.1 %collective-permute-done.2 = bf16[128,3072]{0,1:T(8,128)(2,1)} collective-permute-done((bf16[128,3072]{0,1:T(8,128)(2,1)}, bf16[128,3072]{0,1:T(8,128)(2,1)}, u32[]{:S(2)}, u32[]{:S(2)}) %collective-permute-start.2) | collective-permute-done | bytes 786464 | tf_op jit(solution)/shard_map/ppermute | solution.py:122
  141.5 1.3 constant_dynamic-update-slice_fusion.5
  142.8 12.5 %collective-permute-done.3 = bf16[128,3072]{0,1:T(8,128)(2,1)} collective-permute-done((bf16[128,3072]{0,1:T(8,128)(2,1)}, bf16[128,3072]{0,1:T(8,128)(2,1)}, u32[]{:S(2)}, u32[]{:S(2)}) %collective-permute-start.3) | collective-permute-done | bytes 786464 | tf_op jit(solution)/shard_map/ppermute | solution.py:122
  155.4 1.3 constant_dynamic-update-slice_fusion.4
  157.3 2.4 %collective-permute-start.6 = (f32[1,256,256]{1,2,0:T(8,128)S(1)}, f32[1,256,256]{1,2,0:T(8,128)S(1)}, u32[]{:S(2)}, u32[]{:S(2)}) collective-permute-start(f32[1,256,256]{1,2,0:T(8,128)S(1)} %bitcast.124), channel_id=1, source_target_pairs={{0,12},{8,4},{16,0},{24,8},{28,16},{20,24},{12,28},{4,20},{1,13},{... | collective-permute-start | bytes 786440 | tf_op jit(solution)/shard_map/ppermute | solution.py:152
  161.1 7.4 %collective-permute-done.9 = bf16[128,3072]{0,1:T(8,128)(2,1)} collective-permute-done((bf16[128,3072]{0,1:T(8,128)(2,1)}, bf16[128,3072]{0,1:T(8,128)(2,1)}, u32[]{:S(2)}, u32[]{:S(2)}) %collective-permute-start.9) | collective-permute-done | bytes 786464 | tf_op jit(solution)/shard_map/ppermute | solution.py:124
  168.5 2.7 %fusion.23 = f32[1,256,256]{2,1,0:T(8,128)} fusion(bf16[256,3072]{0,1:T(8,128)(2,1)S(1)} %constant_dynamic-update-slice_fusion.4, bf16[128,3072]{0,1:T(8,128)(2,1)} %collective-permute-done.10, bf16[128,3072]{0,1:T(8,128)(2,1)} %collective-permute-done.9), kind=kOutput, calls=%fused_computation.26 | convolution fusion | flops 405798912 | bytes 3407872 | tf_op jit(solution)/shard_map/dot_general | solution.py:134
  171.2 7.8 %collective-permute-start.11 = (f32[1,256,256]{2,1,0:T(8,128)}, f32[1,256,256]{2,1,0:T(8,128)}, u32[]{:S(2)}, u32[]{:S(2)}) collective-permute-start(f32[1,256,256]{2,1,0:T(8,128)} %fusion.23), channel_id=1, source_target_pairs={{0,16},{8,24},{16,28},{24,20},{28,12},{20,4},{12,0},{4,8},{1,17},{... | collective-permute-start | bytes 786440 | tf_op jit(solution)/shard_map/ppermute | solution.py:152
  179.7 1.1 copy.25
  181.0 6.7 %collective-permute-done.11 = f32[1,256,256]{2,1,0:T(8,128)} collective-permute-done((f32[1,256,256]{2,1,0:T(8,128)}, f32[1,256,256]{2,1,0:T(8,128)}, u32[]{:S(2)}, u32[]{:S(2)}) %collective-permute-start.11) | collective-permute-done | bytes 262176 | tf_op jit(solution)/shard_map/ppermute | solution.py:152
  187.7 1.0 bitcast_dynamic-update-slice_fusion
  188.9 2.7 %collective-permute-done.12 = f32[2,512,256]{2,1,0:T(8,128)} collective-permute-done((f32[2,512,256]{2,1,0:T(8,128)S(1)}, f32[2,512,256]{2,1,0:T(8,128)}, u32[]{:S(2)}, u32[]{:S(2)}) %collective-permute-start.12) | collective-permute-done | bytes 1048608 | tf_op jit(solution)/shard_map/ppermute | solution.py:63
  191.6 1.4 bitcast_add_fusion
  193.1 1.6 collective-permute-start.13
  194.6 12.5 %collective-permute-done.13 = f32[512,256]{1,0:T(8,128)S(1)} collective-permute-done((f32[512,256]{1,0:T(8,128)S(1)}, f32[512,256]{1,0:T(8,128)S(1)}, u32[]{:S(2)}, u32[]{:S(2)}) %collective-permute-start.13) | collective-permute-done | bytes 524320 | tf_op jit(solution)/shard_map/ppermute | solution.py:63
  (61 shorter events, 11.3 us)
Async XLA Ops:
  0.0 68.2 %copy-start = (bf16[1,64,64]{2,1,0:T(8,128)(2,1)S(1)}, bf16[1,64,64]{2,1,0:T(8,128)(2,1)}, u32[]{:S(2)}) copy-start(bf16[1,64,64]{2,1,0:T(8,128)(2,1)} %param.9) | copy-start | bytes 24580
  0.0 3.2 %copy-start.1 = (s32[32]{0:T(128)S(1)}, s32[32]{0:T(128)}, u32[]{:S(2)}) copy-start(s32[32]{0:T(128)} %param.13) | copy-start | bytes 388
  4.7 1.1 copy-start.7
  29.1 30.0 %copy-start.8 = (s32[8]{0:T(128)S(1)}, s32[8]{0:T(128)}, u32[]{:S(2)}) copy-start(s32[8]{0:T(128)} %constant.133.clone) | copy-start | bytes 100
  29.1 37.2 %copy-start.6 = (s32[8]{0:T(128)S(1)}, s32[8]{0:T(128)}, u32[]{:S(2)}) copy-start(s32[8]{0:T(128)} %constant.134.clone) | copy-start | bytes 100
  55.0 30.1 %all-to-all-start.1 = ((bf16[8,16,3072]{2,0,1:T(8,128)(2,1)}), bf16[8,16,3072]{2,0,1:T(8,128)(2,1)S(1)}, u32[]{:S(2)}, u32[]{:S(2)}) async-start(bf16[8,16,3072]{2,0,1:T(8,128)(2,1)} %bitcast.15), calls=%async_computation.1 | async-start | bytes 1572864 | tf_op jit(solution)/shard_map/all_to_all | solution.py:111
  80.9 20.8 %collective-permute-start = (bf16[128,3072]{0,1:T(8,128)(2,1)}, bf16[128,3072]{0,1:T(8,128)(2,1)}, u32[]{:S(2)}, u32[]{:S(2)}) collective-permute-start(bf16[128,3072]{0,1:T(8,128)(2,1)} %reshape.110), channel_id=1, source_target_pairs={{0,8},{8,16},{16,24},{24,28},{28,20},{20,12},{12,4},{4,0},{1,9},{9... | collective-permute-start | bytes 2359304 | tf_op jit(solution)/shard_map/ppermute | solution.py:122
  80.9 22.1 %collective-permute-start.4 = (bf16[128,3072]{0,1:T(8,128)(2,1)}, bf16[128,3072]{0,1:T(8,128)(2,1)}, u32[]{:S(2)}, u32[]{:S(2)}) collective-permute-start(bf16[128,3072]{0,1:T(8,128)(2,1)} %reshape.110), channel_id=1, source_target_pairs={{0,4},{8,0},{16,8},{24,16},{28,24},{20,28},{12,20},{4,12},{1,5},{9... | collective-permute-start | bytes 2359304 | tf_op jit(solution)/shard_map/ppermute | solution.py:124
  95.0 21.4 %collective-permute-start.1 = (bf16[128,3072]{0,1:T(8,128)(2,1)S(1)}, bf16[128,3072]{0,1:T(8,128)(2,1)}, u32[]{:S(2)}, u32[]{:S(2)}) collective-permute-start(bf16[128,3072]{0,1:T(8,128)(2,1)S(1)} %reshape.114), channel_id=1, source_target_pairs={{0,8},{8,16},{16,24},{24,28},{28,20},{20,12},{12,4},{4,0},{1,9},{9... | collective-permute-start | bytes 2359304 | tf_op jit(solution)/shard_map/ppermute | solution.py:122
  95.1 22.7 %collective-permute-start.5 = (bf16[128,3072]{0,1:T(8,128)(2,1)S(1)}, bf16[128,3072]{0,1:T(8,128)(2,1)S(1)}, u32[]{:S(2)}, u32[]{:S(2)}) collective-permute-start(bf16[128,3072]{0,1:T(8,128)(2,1)S(1)} %reshape.114), channel_id=1, source_target_pairs={{0,4},{8,0},{16,8},{24,16},{28,24},{20,28},{12,20},{4,12},{1,5},{9... | collective-permute-start | bytes 2359304 | tf_op jit(solution)/shard_map/ppermute | solution.py:124
  117.8 0.9 copy-start.2
  118.0 2.7 %copy-start.3 = (bf16[256,3072]{0,1:T(8,128)(2,1)}, bf16[256,3072]{0,1:T(8,128)(2,1)S(1)}, u32[]{:S(2)}) copy-start(bf16[256,3072]{0,1:T(8,128)(2,1)S(1)} %constant_dynamic-update-slice_fusion.6) | copy-start | bytes 4718596
  120.7 20.8 %collective-permute-start.2 = (bf16[128,3072]{0,1:T(8,128)(2,1)}, bf16[128,3072]{0,1:T(8,128)(2,1)}, u32[]{:S(2)}, u32[]{:S(2)}) collective-permute-start(bf16[128,3072]{0,1:T(8,128)(2,1)} %collective-permute-done), channel_id=1, source_target_pairs={{0,8},{8,16},{16,24},{24,28},{28,20},{20,12},{12,4},{4,0},{1,9},{9... | collective-permute-start | bytes 2359304 | tf_op jit(solution)/shard_map/ppermute | solution.py:122
  121.1 15.0 %collective-permute-start.7 = (f32[2,256,256]{1,2,0:T(8,128)S(1)}, f32[2,256,256]{1,2,0:T(8,128)}, u32[]{:S(2)}, u32[]{:S(2)}) collective-permute-start(f32[2,256,256]{1,2,0:T(8,128)S(1)} %pad_maximum_fusion), channel_id=1, source_target_pairs={{0,4},{8,0},{16,8},{24,16},{28,24},{20,28},{12,20},{4,12},{1,5},{9... | collective-permute-start | bytes 1572872 | tf_op jit(solution)/shard_map/ppermute | solution.py:152
  122.9 32.5 %collective-permute-start.3 = (bf16[128,3072]{0,1:T(8,128)(2,1)}, bf16[128,3072]{0,1:T(8,128)(2,1)}, u32[]{:S(2)}, u32[]{:S(2)}) collective-permute-start(bf16[128,3072]{0,1:T(8,128)(2,1)} %collective-permute-done.1), channel_id=1, source_target_pairs={{0,8},{8,16},{16,24},{24,28},{28,20},{20,12},{12,4},{4,0},{1,9},{9... | collective-permute-start | bytes 2359304 | tf_op jit(solution)/shard_map/ppermute | solution.py:122
  127.0 34.1 %collective-permute-start.10 = (bf16[128,3072]{0,1:T(8,128)(2,1)}, bf16[128,3072]{0,1:T(8,128)(2,1)}, u32[]{:S(2)}, u32[]{:S(2)}) collective-permute-start(bf16[128,3072]{0,1:T(8,128)(2,1)} %copy-done.2), channel_id=1, source_target_pairs={{0,4},{8,0},{16,8},{24,16},{28,24},{20,28},{12,20},{4,12},{1,5},{9... | collective-permute-start | bytes 2359304 | tf_op jit(solution)/shard_map/ppermute | solution.py:124
  128.8 39.7 %collective-permute-start.9 = (bf16[128,3072]{0,1:T(8,128)(2,1)}, bf16[128,3072]{0,1:T(8,128)(2,1)}, u32[]{:S(2)}, u32[]{:S(2)}) collective-permute-start(bf16[128,3072]{0,1:T(8,128)(2,1)} %collective-permute-done.4), channel_id=1, source_target_pairs={{0,4},{8,0},{16,8},{24,16},{28,24},{20,28},{12,20},{4,12},{1,5},{9... | collective-permute-start | bytes 2359304 | tf_op jit(solution)/shard_map/ppermute | solution.py:124
  137.5 19.2 %copy-start.4 = (bf16[256,3072]{0,1:T(8,128)(2,1)S(1)}, bf16[256,3072]{0,1:T(8,128)(2,1)}, u32[]{:S(2)}) copy-start(bf16[256,3072]{0,1:T(8,128)(2,1)} %copy-done.3) | copy-start | bytes 4718596
  157.3 21.7 %collective-permute-start.6 = (f32[1,256,256]{1,2,0:T(8,128)S(1)}, f32[1,256,256]{1,2,0:T(8,128)S(1)}, u32[]{:S(2)}, u32[]{:S(2)}) collective-permute-start(f32[1,256,256]{1,2,0:T(8,128)S(1)} %bitcast.124), channel_id=1, source_target_pairs={{0,12},{8,4},{16,0},{24,8},{28,16},{20,24},{12,28},{4,20},{1,13},{... | collective-permute-start | bytes 786440 | tf_op jit(solution)/shard_map/ppermute | solution.py:152
  160.5 20.4 %collective-permute-start.8 = (f32[2,256,256]{2,1,0:T(8,128)}, f32[2,256,256]{2,1,0:T(8,128)S(1)}, u32[]{:S(2)}, u32[]{:S(2)}) collective-permute-start(f32[2,256,256]{2,1,0:T(8,128)} %pad_maximum_fusion.1), channel_id=1, source_target_pairs={{0,8},{8,16},{16,24},{24,28},{28,20},{20,12},{12,4},{4,0},{1,9},{9... | collective-permute-start | bytes 1572872 | tf_op jit(solution)/shard_map/ppermute | solution.py:152
  171.2 16.5 %collective-permute-start.11 = (f32[1,256,256]{2,1,0:T(8,128)}, f32[1,256,256]{2,1,0:T(8,128)}, u32[]{:S(2)}, u32[]{:S(2)}) collective-permute-start(f32[1,256,256]{2,1,0:T(8,128)} %fusion.23), channel_id=1, source_target_pairs={{0,16},{8,24},{16,28},{24,20},{28,12},{20,4},{12,0},{4,8},{1,17},{... | collective-permute-start | bytes 786440 | tf_op jit(solution)/shard_map/ppermute | solution.py:152
  179.0 0.7 copy-start.5
  188.8 2.9 %collective-permute-start.12 = (f32[2,512,256]{2,1,0:T(8,128)S(1)}, f32[2,512,256]{2,1,0:T(8,128)}, u32[]{:S(2)}, u32[]{:S(2)}) collective-permute-start(f32[2,512,256]{2,1,0:T(8,128)S(1)} %dynamic-slice_bitcast_fusion), channel_id=1, source_target_pairs={{0,1},{1,0},{2,3},{3,2},{4,5},{5,4},{6,7},{7,6},{8,9},{9,8},{10,11... | collective-permute-start | bytes 3145736 | tf_op jit(solution)/shard_map/ppermute | solution.py:63
  193.1 14.0 %collective-permute-start.13 = (f32[512,256]{1,0:T(8,128)S(1)}, f32[512,256]{1,0:T(8,128)S(1)}, u32[]{:S(2)}, u32[]{:S(2)}) collective-permute-start(f32[512,256]{1,0:T(8,128)S(1)} %dynamic-slice_bitcast_fusion.1), channel_id=1, source_target_pairs={{0,2},{1,3},{2,0},{3,1},{4,6},{5,7},{6,4},{7,5},{8,10},{9,11},{10,... | collective-permute-start | bytes 1572872 | tf_op jit(solution)/shard_map/ppermute | solution.py:63
where the time goes:
time: 209 us; the launch traced here: 208 us
  waiting for transfers between devices  65 us (31%)
  local copies, waits for them, and re-layouts  54.5 us (26%)
  starting transfers between devices  26.3 us (13%)
  blocking collectives  25.8 us (12%)
  matrix products  17.2 us (8%)
  between operations  12.1 us (6%)
  other arithmetic  6.92 us (3%)
    ppermute x4, waiting for transfers between devices, body(): fwd = lax.ppermute(fwd, 'grp', shifted(1))  29.8 us
    all_to_all x1, blocking collectives, body(): lax.all_to_all(part, 'grp', split_axis=1, concat_axis=0, tiled=True)  25.8 us
    ppermute x2, waiting for transfers between devices, scatter_sum(): got = lax.ppermute(send, 'rep', [(i, i ^ d) for i in range(n_rep)])  15.2 us
    unnamed x23, local copies, waits for them, and re-layouts  14.1 us
    ppermute x4, waiting for transfers between devices, body(): got = lax.ppermute(stack, 'grp', shifted(s))  12.6 us
    ppermute x4, starting transfers between devices, body(): got = lax.ppermute(stack, 'grp', shifted(s))  12.5 us
    transpose x2, local copies, waits for them, and re-layouts, body(): jnp.transpose(mixed, (1, 2, 0, 3)).reshape(mu_c * NB, n_aux * n_occ)  8.5 us
    dot_general x5, matrix products, prod(): return jnp.dot(held[xo], held[yo].T, preferred_element_type=jnp.float32)  8.43 us
  transfers between devices with their start and end apart: 15, of which 9 were waited for; matrix products, arithmetic and copies ran while one was open for 21% of the time, Pallas kernels for 0%

commit v1 on v0

--- a/solution.py
+++ b/solution.py
@@ -108,7 +108,12 @@
         helds = []
         for h in range(n_split):
             part = half[:, :, h * mu_c : (h + 1) * mu_c].reshape(aux_dev, n * mu_c, NB * n_occ)
-            regrouped = lax.all_to_all(part, "grp", split_axis=1, concat_axis=0, tiled=True)
+            regrouped = jnp.concatenate(
+                lax.all_to_all(
+                    jnp.stack(jnp.split(part, lax.axis_size("grp"), axis=1)), "grp", 0, 0
+                ),
+                axis=0,
+            )
             n_aux = regrouped.shape[0]
             mixed = jnp.dot(
                 metric[0], regrouped.reshape(n_aux, -1), preferred_element_type=jnp.float32

time: 209 us -> 217 us (1.038)
  blocking collectives: 25.8 us -> 0 us
  waiting for transfers between devices: 65 us -> 89.5 us
  starting transfers between devices: 26.3 us -> 32.9 us
  local copies, waits for them, and re-layouts: 54.5 us -> 59.6 us
  matrix products: 17.2 us -> 14.7 us
    all_to_all x1 -> x0, blocking collectives: 25.8 us -> none  [body(): lax.all_to_all(part, 'grp', split_axis=1, concat_axis=0, tiled=True)]
    all_to_all x1 -> x2, waiting for transfers between devices: 0.01 us -> 18.5 us  [body(): lax.all_to_all(jnp.stack(jnp.split(part, lax.axis_size('grp'), axis=1)),...]
    ppermute x4, waiting for transfers between devices: 7.43 us -> 25.2 us  [body(): bwd = lax.ppermute(bwd, 'grp', shifted(-1))]
    ppermute x4, waiting for transfers between devices: 29.8 us -> 17.8 us  [body(): fwd = lax.ppermute(fwd, 'grp', shifted(1))]
    all_to_all x1 -> x2, starting transfers between devices: 4.15 us -> 10.7 us  [body(): lax.all_to_all(jnp.stack(jnp.split(part, lax.axis_size('grp'), axis=1)),...]
    dot_general x5, matrix products: 8.43 us -> 5.13 us  [prod(): return jnp.dot(held[xo], held[yo].T, preferred_element_type=jnp.float32)]
    unnamed x23 -> x39, local copies, waits for them, and re-layouts: 14.1 us -> 16.3 us
  transfers between devices with their start and end apart: 15 -> 16, of which waited for: 9 -> 10; matrix products, arithmetic and copies ran while one was open for 21% -> 19% of each run, Pallas kernels for 0% -> 0%
where the time goes in v1:
time: 217 us; the launch traced here: 216 us
  waiting for transfers between devices  89.5 us (41%)
  local copies, waits for them, and re-layouts  59.6 us (27%)
  starting transfers between devices  32.9 us (15%)
  matrix products  14.7 us (7%)
  between operations  12.1 us (6%)
  other arithmetic  6.9 us (3%)
    ppermute x4, waiting for transfers between devices, body(): bwd = lax.ppermute(bwd, 'grp', shifted(-1))  25.2 us
    all_to_all x2, waiting for transfers between devices, body(): lax.all_to_all(jnp.stack(jnp.split(part, lax.axis_size('grp'), axis=1)),...  18.5 us
    ppermute x4, waiting for transfers between devices, body(): fwd = lax.ppermute(fwd, 'grp', shifted(1))  17.8 us
    unnamed x39, local copies, waits for them, and re-layouts  16.3 us
    ppermute x2, waiting for transfers between devices, scatter_sum(): got = lax.ppermute(send, 'rep', [(i, i ^ d) for i in range(n_rep)])  15.2 us
    ppermute x4, waiting for transfers between devices, body(): got = lax.ppermute(stack, 'grp', shifted(s))  12.8 us
    ppermute x4, starting transfers between devices, body(): got = lax.ppermute(stack, 'grp', shifted(s))  12.3 us
    all_to_all x2, starting transfers between devices, body(): lax.all_to_all(jnp.stack(jnp.split(part, lax.axis_size('grp'), axis=1)),...  10.7 us
  transfers between devices with their start and end apart: 16, of which 10 were waited for; matrix products, arithmetic and copies ran while one was open for 19% of the time, Pallas kernels for 0%

profile of v1, /device:TPU:2, one launch (start us, length us, event | category | flops | bytes accessed | tf_op | source)
XLA Modules:
  0.0 215.9 jit_solution(6538772136948504101)
XLA Ops:
  0.9 1.3 reshape.96
  3.2 1.6 gather_fusion
  4.7 1.0 gather_fusion.1
  5.9 7.4 %copy.30 = bf16[192,8,32,128]{3,2,1,0:T(8,128)(2,1)S(1)} copy(bf16[192,8,32,128]{3,1,2,0:T(8,128)(2,1)} %bitcast.168) | data formatting | bytes 25165824
  13.5 1.6 broadcast_select_fusion
  15.1 7.1 %fusion.14 = bf16[8,32,32,96]{3,2,0,1:T(8,128)(2,1)} fusion(bf16[8,6,32,32,128]{4,3,2,1,0:T(8,128)(2,1)S(1)} %bitcast.169, bf16[32,6,64,48]{2,3,1,0:T(8,128)(2,1)} %broadcast_select_fusion), kind=kOutput, calls=%fused_computation.20 | convolution fusion | flops 1226833920 | bytes 15335424 | tf_op jit(solution)/shard_map/qkmtl,mklc->qmtc/dot_general | solution.py:97
  22.2 4.2 %reshape.98 = bf16[8,8,4,3072]{3,0,2,1:T(8,128)(2,1)S(1)} reshape(bf16[8,32,32,96]{3,2,0,1:T(8,128)(2,1)} %fusion.14) | data formatting | bytes 3145728 | tf_op jit(solution)/shard_map/reshape | solution.py:98
  33.3 6.5 %all-to-all-start.1 = ((bf16[8,8,2,3072]{3,1,2,0:T(8,128)(2,1)}), bf16[8,8,2,3072]{3,1,2,0:T(8,128)(2,1)S(1)}, u32[]{:S(2)}, u32[]{:S(2)}) async-start(bf16[8,8,2,3072]{3,1,2,0:T(8,128)(2,1)} %fusion.29), calls=%async_computation.1 | async-start | bytes 1572864 | tf_op jit(solution)/shard_map/all_to_all | solution.py:112
  39.9 0.9 copy-done.2
  40.8 18.5 %all-to-all-done.1 = bf16[8,8,2,3072]{3,1,2,0:T(8,128)(2,1)S(1)} async-done(((bf16[8,8,2,3072]{3,1,2,0:T(8,128)(2,1)}), bf16[8,8,2,3072]{3,1,2,0:T(8,128)(2,1)S(1)}, u32[]{:S(2)}, u32[]{:S(2)}) %all-to-all-start.1) | async-done | bytes 786464 | tf_op jit(solution)/shard_map/all_to_all | solution.py:112
  59.3 4.2 %all-to-all-start = ((bf16[8,8,2,3072]{3,1,2,0:T(8,128)(2,1)}), bf16[8,8,2,3072]{3,1,2,0:T(8,128)(2,1)S(1)}, u32[]{:S(2)}, u32[]{:S(2)}) async-start(bf16[8,8,2,3072]{3,1,2,0:T(8,128)(2,1)} %copy-done.2), calls=%async_computation | async-start | bytes 1572864 | tf_op jit(solution)/shard_map/all_to_all | solution.py:112
  72.7 1.2 fusion.5
  73.9 3.3 %reshape.103 = bf16[64,2,64,48]{3,2,1,0:T(8,128)(2,1)S(1)} reshape(bf16[64,6144]{1,0:T(8,128)(2,1)} %fusion.5) | data formatting | bytes 1572864 | tf_op jit(solution)/shard_map/reshape | solution.py:121
  77.2 4.3 %copy.24 = bf16[2,64,64,48]{1,0,3,2:T(2,128)(2,1)} copy(bf16[2,64,64,48]{3,1,0,2:T(8,128)(2,1)S(1)} %bitcast.172) | data formatting | bytes 1572864 | tf_op jit(solution)/shard_map/transpose | solution.py:122
  81.5 3.9 %reshape.104 = bf16[128,3072]{0,1:T(8,128)(2,1)} reshape(bf16[2,64,64,48]{1,0,3,2:T(2,128)(2,1)} %copy.24) | data formatting | bytes 1572864 | tf_op jit(solution)/shard_map/reshape | solution.py:122
  85.3 1.5 collective-permute-start.5
  87.4 1.2 fusion.4
  88.6 3.3 %reshape.100 = bf16[64,2,64,48]{3,2,1,0:T(8,128)(2,1)S(1)} reshape(bf16[64,6144]{1,0:T(8,128)(2,1)} %fusion.4) | data formatting | bytes 1572864 | tf_op jit(solution)/shard_map/reshape | solution.py:121
  91.9 4.3 %copy.23 = bf16[2,64,64,48]{1,0,3,2:T(2,128)(2,1)} copy(bf16[2,64,64,48]{3,1,0,2:T(8,128)(2,1)S(1)} %bitcast.173) | data formatting | bytes 1572864 | tf_op jit(solution)/shard_map/transpose | solution.py:122
  96.1 3.1 %reshape.101 = bf16[128,3072]{0,1:T(8,128)(2,1)S(1)} reshape(bf16[2,64,64,48]{1,0,3,2:T(2,128)(2,1)} %copy.23) | data formatting | bytes 1572864 | tf_op jit(solution)/shard_map/reshape | solution.py:122
  99.3 1.5 collective-permute-start.4
  101.5 1.3 constant_dynamic-update-slice_fusion
  103.6 17.7 %collective-permute-done.4 = bf16[128,3072]{0,1:T(8,128)(2,1)S(1)} collective-permute-done((bf16[128,3072]{0,1:T(8,128)(2,1)S(1)}, bf16[128,3072]{0,1:T(8,128)(2,1)S(1)}, u32[]{:S(2)}, u32[]{:S(2)}) %collective-permute-start.4) | collective-permute-done | bytes 786464 | tf_op jit(solution)/shard_map/ppermute | solution.py:129
  121.4 1.1 collective-permute-done
  122.6 1.3 constant_dynamic-update-slice_fusion.3
  123.9 1.3 constant_dynamic-update-slice_fusion.6
  125.2 1.9 constant_dynamic-update-slice_fusion.2
  129.0 1.5 collective-permute-start.7
  134.9 1.5 collective-permute-start.10
  136.4 1.5 collective-permute-start.9
  137.8 6.2 %collective-permute-done.7 = f32[2,256,256]{1,2,0:T(8,128)} collective-permute-done((f32[2,256,256]{1,2,0:T(8,128)S(1)}, f32[2,256,256]{1,2,0:T(8,128)}, u32[]{:S(2)}, u32[]{:S(2)}) %collective-permute-start.7) | collective-permute-done | bytes 524320 | tf_op jit(solution)/shard_map/ppermute | solution.py:157
  144.0 1.1 slice_bitcast_fusion.2
  145.4 3.8 %collective-permute-done.2 = bf16[128,3072]{0,1:T(8,128)(2,1)} collective-permute-done((bf16[128,3072]{0,1:T(8,128)(2,1)}, bf16[128,3072]{0,1:T(8,128)(2,1)}, u32[]{:S(2)}, u32[]{:S(2)}) %collective-permute-start.2) | collective-permute-done | bytes 786464 | tf_op jit(solution)/shard_map/ppermute | solution.py:127
  149.2 1.3 constant_dynamic-update-slice_fusion.5
  150.5 12.8 %collective-permute-done.3 = bf16[128,3072]{0,1:T(8,128)(2,1)} collective-permute-done((bf16[128,3072]{0,1:T(8,128)(2,1)}, bf16[128,3072]{0,1:T(8,128)(2,1)}, u32[]{:S(2)}, u32[]{:S(2)}) %collective-permute-start.3) | collective-permute-done | bytes 786464 | tf_op jit(solution)/shard_map/ppermute | solution.py:127
  163.3 1.3 constant_dynamic-update-slice_fusion.4
  166.6 2.4 %collective-permute-start.6 = (f32[1,256,256]{1,2,0:T(8,128)S(1)}, f32[1,256,256]{1,2,0:T(8,128)S(1)}, u32[]{:S(2)}, u32[]{:S(2)}) collective-permute-start(f32[1,256,256]{1,2,0:T(8,128)S(1)} %bitcast.196), channel_id=1, source_target_pairs={{0,12},{8,4},{16,0},{24,8},{28,16},{20,24},{12,28},{4,20},{1,13},{... | collective-permute-start | bytes 786440 | tf_op jit(solution)/shard_map/ppermute | solution.py:157
  169.0 7.5 %collective-permute-done.9 = bf16[128,3072]{0,1:T(8,128)(2,1)} collective-permute-done((bf16[128,3072]{0,1:T(8,128)(2,1)}, bf16[128,3072]{0,1:T(8,128)(2,1)}, u32[]{:S(2)}, u32[]{:S(2)}) %collective-permute-start.9) | collective-permute-done | bytes 786464 | tf_op jit(solution)/shard_map/ppermute | solution.py:129
  176.5 2.7 %fusion.23 = f32[1,256,256]{2,1,0:T(8,128)} fusion(bf16[256,3072]{0,1:T(8,128)(2,1)S(1)} %constant_dynamic-update-slice_fusion.4, bf16[128,3072]{0,1:T(8,128)(2,1)} %collective-permute-done.10, bf16[128,3072]{0,1:T(8,128)(2,1)} %collective-permute-done.9), kind=kOutput, calls=%fused_computation.26 | convolution fusion | flops 405798912 | bytes 3407872 | tf_op jit(solution)/shard_map/dot_general | solution.py:139
  179.2 7.9 %collective-permute-start.11 = (f32[1,256,256]{2,1,0:T(8,128)}, f32[1,256,256]{2,1,0:T(8,128)}, u32[]{:S(2)}, u32[]{:S(2)}) collective-permute-start(f32[1,256,256]{2,1,0:T(8,128)} %fusion.23), channel_id=1, source_target_pairs={{0,16},{8,24},{16,28},{24,20},{28,12},{20,4},{12,0},{4,8},{1,17},{... | collective-permute-start | bytes 786440 | tf_op jit(solution)/shard_map/ppermute | solution.py:157
  187.8 1.1 copy.25
  189.1 6.6 %collective-permute-done.11 = f32[1,256,256]{2,1,0:T(8,128)} collective-permute-done((f32[1,256,256]{2,1,0:T(8,128)}, f32[1,256,256]{2,1,0:T(8,128)}, u32[]{:S(2)}, u32[]{:S(2)}) %collective-permute-start.11) | collective-permute-done | bytes 262176 | tf_op jit(solution)/shard_map/ppermute | solution.py:157
  195.6 1.0 bitcast_dynamic-update-slice_fusion
  196.8 2.7 %collective-permute-done.12 = f32[2,512,256]{2,1,0:T(8,128)} collective-permute-done((f32[2,512,256]{2,1,0:T(8,128)S(1)}, f32[2,512,256]{2,1,0:T(8,128)}, u32[]{:S(2)}, u32[]{:S(2)}) %collective-permute-start.12) | collective-permute-done | bytes 1048608 | tf_op jit(solution)/shard_map/ppermute | solution.py:63
  199.5 1.4 bitcast_add_fusion
  201.0 1.6 collective-permute-start.13
  202.5 12.4 %collective-permute-done.13 = f32[512,256]{1,0:T(8,128)S(1)} collective-permute-done((f32[512,256]{1,0:T(8,128)S(1)}, f32[512,256]{1,0:T(8,128)S(1)}, u32[]{:S(2)}, u32[]{:S(2)}) %collective-permute-start.13) | collective-permute-done | bytes 524320 | tf_op jit(solution)/shard_map/ppermute | solution.py:63
  215.0 0.9 bitcast_add_fusion.1
  (80 shorter events, 18.2 us)
Async XLA Ops:
  0.0 72.7 %copy-start = (bf16[1,64,64]{2,1,0:T(8,128)(2,1)S(1)}, bf16[1,64,64]{2,1,0:T(8,128)(2,1)}, u32[]{:S(2)}) copy-start(bf16[1,64,64]{2,1,0:T(8,128)(2,1)} %param.9) | copy-start | bytes 24580
  0.0 3.2 %copy-start.1 = (s32[32]{0:T(128)S(1)}, s32[32]{0:T(128)}, u32[]{:S(2)}) copy-start(s32[32]{0:T(128)} %param.13) | copy-start | bytes 388
  4.7 1.1 copy-start.8
  33.3 30.2 %copy-start.9 = (s32[8]{0:T(128)S(1)}, s32[8]{0:T(128)}, u32[]{:S(2)}) copy-start(s32[8]{0:T(128)} %constant.133.clone) | copy-start | bytes 100
  33.3 37.4 %copy-start.7 = (s32[8]{0:T(128)S(1)}, s32[8]{0:T(128)}, u32[]{:S(2)}) copy-start(s32[8]{0:T(128)} %constant.134.clone) | copy-start | bytes 100
  33.3 26.0 %all-to-all-start.1 = ((bf16[8,8,2,3072]{3,1,2,0:T(8,128)(2,1)}), bf16[8,8,2,3072]{3,1,2,0:T(8,128)(2,1)S(1)}, u32[]{:S(2)}, u32[]{:S(2)}) async-start(bf16[8,8,2,3072]{3,1,2,0:T(8,128)(2,1)} %fusion.29), calls=%async_computation.1 | async-start | bytes 1572864 | tf_op jit(solution)/shard_map/all_to_all | solution.py:112
  39.9 0.9 copy-start.2
  59.3 28.1 %all-to-all-start = ((bf16[8,8,2,3072]{3,1,2,0:T(8,128)(2,1)}), bf16[8,8,2,3072]{3,1,2,0:T(8,128)(2,1)S(1)}, u32[]{:S(2)}, u32[]{:S(2)}) async-start(bf16[8,8,2,3072]{3,1,2,0:T(8,128)(2,1)} %copy-done.2), calls=%async_computation | async-start | bytes 1572864 | tf_op jit(solution)/shard_map/all_to_all | solution.py:112
  85.3 38.5 %collective-permute-start.5 = (bf16[128,3072]{0,1:T(8,128)(2,1)}, bf16[128,3072]{0,1:T(8,128)(2,1)}, u32[]{:S(2)}, u32[]{:S(2)}) collective-permute-start(bf16[128,3072]{0,1:T(8,128)(2,1)} %reshape.104), channel_id=1, source_target_pairs={{0,4},{8,0},{16,8},{24,16},{28,24},{20,28},{12,20},{4,12},{1,5},{9... | collective-permute-start | bytes 2359304 | tf_op jit(solution)/shard_map/ppermute | solution.py:129
  86.8 38.4 %collective-permute-start.1 = (bf16[128,3072]{0,1:T(8,128)(2,1)}, bf16[128,3072]{0,1:T(8,128)(2,1)}, u32[]{:S(2)}, u32[]{:S(2)}) collective-permute-start(bf16[128,3072]{0,1:T(8,128)(2,1)} %reshape.104), channel_id=1, source_target_pairs={{0,8},{8,16},{16,24},{24,28},{28,20},{20,12},{12,4},{4,0},{1,9},{9... | collective-permute-start | bytes 2359304 | tf_op jit(solution)/shard_map/ppermute | solution.py:127
  99.3 22.0 %collective-permute-start.4 = (bf16[128,3072]{0,1:T(8,128)(2,1)S(1)}, bf16[128,3072]{0,1:T(8,128)(2,1)S(1)}, u32[]{:S(2)}, u32[]{:S(2)}) collective-permute-start(bf16[128,3072]{0,1:T(8,128)(2,1)S(1)} %reshape.101), channel_id=1, source_target_pairs={{0,4},{8,0},{16,8},{24,16},{28,24},{20,28},{12,20},{4,12},{1,5},{9... | collective-permute-start | bytes 2359304 | tf_op jit(solution)/shard_map/ppermute | solution.py:129
  100.8 21.8 %collective-permute-start = (bf16[128,3072]{0,1:T(8,128)(2,1)S(1)}, bf16[128,3072]{0,1:T(8,128)(2,1)}, u32[]{:S(2)}, u32[]{:S(2)}) collective-permute-start(bf16[128,3072]{0,1:T(8,128)(2,1)S(1)} %reshape.101), channel_id=1, source_target_pairs={{0,8},{8,16},{16,24},{24,28},{28,20},{20,12},{12,4},{4,0},{1,9},{9... | collective-permute-start | bytes 2359304 | tf_op jit(solution)/shard_map/ppermute | solution.py:127
  121.3 7.1 %copy-start.3 = (bf16[128,3072]{0,1:T(8,128)(2,1)}, bf16[128,3072]{0,1:T(8,128)(2,1)S(1)}, u32[]{:S(2)}) copy-start(bf16[128,3072]{0,1:T(8,128)(2,1)S(1)} %collective-permute-done.4) | copy-start | bytes 2359300
  125.2 2.5 %copy-start.4 = (bf16[256,3072]{0,1:T(8,128)(2,1)}, bf16[256,3072]{0,1:T(8,128)(2,1)S(1)}, u32[]{:S(2)}) copy-start(bf16[256,3072]{0,1:T(8,128)(2,1)S(1)} %constant_dynamic-update-slice_fusion.6) | copy-start | bytes 4718596
  128.4 20.8 %collective-permute-start.2 = (bf16[128,3072]{0,1:T(8,128)(2,1)}, bf16[128,3072]{0,1:T(8,128)(2,1)}, u32[]{:S(2)}, u32[]{:S(2)}) collective-permute-start(bf16[128,3072]{0,1:T(8,128)(2,1)} %collective-permute-done), channel_id=1, source_target_pairs={{0,8},{8,16},{16,24},{24,28},{28,20},{20,12},{12,4},{4,0},{1,9},{9... | collective-permute-start | bytes 2359304 | tf_op jit(solution)/shard_map/ppermute | solution.py:127
  129.0 15.0 %collective-permute-start.7 = (f32[2,256,256]{1,2,0:T(8,128)S(1)}, f32[2,256,256]{1,2,0:T(8,128)}, u32[]{:S(2)}, u32[]{:S(2)}) collective-permute-start(f32[2,256,256]{1,2,0:T(8,128)S(1)} %pad_maximum_fusion), channel_id=1, source_target_pairs={{0,4},{8,0},{16,8},{24,16},{28,24},{20,28},{12,20},{4,12},{1,5},{9... | collective-permute-start | bytes 1572872 | tf_op jit(solution)/shard_map/ppermute | solution.py:157
  130.5 32.7 %collective-permute-start.3 = (bf16[128,3072]{0,1:T(8,128)(2,1)}, bf16[128,3072]{0,1:T(8,128)(2,1)}, u32[]{:S(2)}, u32[]{:S(2)}) collective-permute-start(bf16[128,3072]{0,1:T(8,128)(2,1)} %collective-permute-done.1), channel_id=1, source_target_pairs={{0,8},{8,16},{16,24},{24,28},{28,20},{20,12},{12,4},{4,0},{1,9},{9... | collective-permute-start | bytes 2359304 | tf_op jit(solution)/shard_map/ppermute | solution.py:127
  134.9 34.1 %collective-permute-start.10 = (bf16[128,3072]{0,1:T(8,128)(2,1)}, bf16[128,3072]{0,1:T(8,128)(2,1)}, u32[]{:S(2)}, u32[]{:S(2)}) collective-permute-start(bf16[128,3072]{0,1:T(8,128)(2,1)} %collective-permute-done.5), channel_id=1, source_target_pairs={{0,4},{8,0},{16,8},{24,16},{28,24},{20,28},{12,20},{4,12},{1,5},{9... | collective-permute-start | bytes 2359304 | tf_op jit(solution)/shard_map/ppermute | solution.py:129
  136.4 40.1 %collective-permute-start.9 = (bf16[128,3072]{0,1:T(8,128)(2,1)}, bf16[128,3072]{0,1:T(8,128)(2,1)}, u32[]{:S(2)}, u32[]{:S(2)}) collective-permute-start(bf16[128,3072]{0,1:T(8,128)(2,1)} %copy-done.3), channel_id=1, source_target_pairs={{0,4},{8,0},{16,8},{24,16},{28,24},{20,28},{12,20},{4,12},{1,5},{9... | collective-permute-start | bytes 2359304 | tf_op jit(solution)/shard_map/ppermute | solution.py:129
  145.4 19.2 %copy-start.5 = (bf16[256,3072]{0,1:T(8,128)(2,1)S(1)}, bf16[256,3072]{0,1:T(8,128)(2,1)}, u32[]{:S(2)}) copy-start(bf16[256,3072]{0,1:T(8,128)(2,1)} %copy-done.4) | copy-start | bytes 4718596
  166.1 22.9 %collective-permute-start.8 = (f32[2,256,256]{2,1,0:T(8,128)}, f32[2,256,256]{2,1,0:T(8,128)S(1)}, u32[]{:S(2)}, u32[]{:S(2)}) collective-permute-start(f32[2,256,256]{2,1,0:T(8,128)} %pad_maximum_fusion.1), channel_id=1, source_target_pairs={{0,8},{8,16},{16,24},{24,28},{28,20},{20,12},{12,4},{4,0},{1,9},{9... | collective-permute-start | bytes 1572872 | tf_op jit(solution)/shard_map/ppermute | solution.py:157
  166.6 20.4 %collective-permute-start.6 = (f32[1,256,256]{1,2,0:T(8,128)S(1)}, f32[1,256,256]{1,2,0:T(8,128)S(1)}, u32[]{:S(2)}, u32[]{:S(2)}) collective-permute-start(f32[1,256,256]{1,2,0:T(8,128)S(1)} %bitcast.196), channel_id=1, source_target_pairs={{0,12},{8,4},{16,0},{24,8},{28,16},{20,24},{12,28},{4,20},{1,13},{... | collective-permute-start | bytes 786440 | tf_op jit(solution)/shard_map/ppermute | solution.py:157
  179.2 16.5 %collective-permute-start.11 = (f32[1,256,256]{2,1,0:T(8,128)}, f32[1,256,256]{2,1,0:T(8,128)}, u32[]{:S(2)}, u32[]{:S(2)}) collective-permute-start(f32[1,256,256]{2,1,0:T(8,128)} %fusion.23), channel_id=1, source_target_pairs={{0,16},{8,24},{16,28},{24,20},{28,12},{20,4},{12,0},{4,8},{1,17},{... | collective-permute-start | bytes 786440 | tf_op jit(solution)/shard_map/ppermute | solution.py:157
  187.1 0.7 copy-start.6
  196.7 2.9 %collective-permute-start.12 = (f32[2,512,256]{2,1,0:T(8,128)S(1)}, f32[2,512,256]{2,1,0:T(8,128)}, u32[]{:S(2)}, u32[]{:S(2)}) collective-permute-start(f32[2,512,256]{2,1,0:T(8,128)S(1)} %dynamic-slice_bitcast_fusion), channel_id=1, source_target_pairs={{0,1},{1,0},{2,3},{3,2},{4,5},{5,4},{6,7},{7,6},{8,9},{9,8},{10,11... | collective-permute-start | bytes 3145736 | tf_op jit(solution)/shard_map/ppermute | solution.py:63
  201.0 14.0 %collective-permute-start.13 = (f32[512,256]{1,0:T(8,128)S(1)}, f32[512,256]{1,0:T(8,128)S(1)}, u32[]{:S(2)}, u32[]{:S(2)}) collective-permute-start(f32[512,256]{1,0:T(8,128)S(1)} %dynamic-slice_bitcast_fusion.1), channel_id=1, source_target_pairs={{0,2},{1,3},{2,0},{3,1},{4,6},{5,7},{6,4},{7,5},{8,10},{9,11},{10,... | collective-permute-start | bytes 1572872 | tf_op jit(solution)/shard_map/ppermute | solution.py:63
